TPU v7x, 32 devices: a whole 2x2x4 slice. The times are simulated.
32 devices in a mesh: ctx: 8 (over y, x, core), tp: 4 (over z).
Axes of the slice: x: 2, y: 2, z: 4, core: 2. Of those that a mesh axis runs over, the one named last changes fastest.
Arguments:
- stream: bfloat16 [1024, 4096], P('ctx', 'tp'), may hold values from -52 to 52
- shutter: bfloat16 [1024, 4096], P('ctx', 'tp'), may hold values from -6 to 6
- feeder: bfloat16 [1024, 4096], P('ctx', 'tp'), may hold values from -6 to 6
- stencil: float32 [7, 4096], P(None, 'tp'), may hold values from -2 to 2
- valves: bfloat16 [1024, 4096], P('ctx', 'tp'), may hold values from -6 to 6
- intake: bfloat16 [1024, 4096], P('ctx', 'tp'), may hold values from -6 to 6
- kernel: float32 [128, 4096], P(None, 'tp'), may hold values from -0.5 to 0.5
- scaling: float32 [4096], P('tp'), may hold values from 0.1 to 1.9
- queries: bfloat16 [1024, 4096], P('ctx', 'tp'), may hold values from -87 to 87
- matchers: bfloat16 [1024, 4096], P('ctx', 'tp'), may hold values from -6 to 6
- segments: int32 [1024], replicated, may hold values from 0 to 3, never falling along the last dimension, each value on 1 to 768 neighbouring positions
- cotangent: bfloat16 [1024, 4096], P('ctx', 'tp'), may hold values from -6 to 6
Outputs:
- result: bfloat16 [1024, 4096], P('ctx', 'tp')
- stream_grad: bfloat16 [1024, 4096], P('ctx', 'tp')
- shutter_grad: bfloat16 [1024, 4096], P('ctx', 'tp')
- feeder_grad: bfloat16 [1024, 4096], P('ctx', 'tp')
- stencil_grad: float32 [7, 4096], P(None, 'tp')
- valves_grad: bfloat16 [1024, 4096], P('ctx', 'tp')
- intake_grad: bfloat16 [1024, 4096], P('ctx', 'tp')
- kernel_grad: float32 [128, 4096], P(None, 'tp')
- scaling_grad: float32 [4096], P('tp')
- queries_grad: bfloat16 [1024, 4096], P('ctx', 'tp')
- matchers_grad: bfloat16 [1024, 4096], P('ctx', 'tp')
Inputs may be any that keep to these rules, and one draw needn't show every extreme that they name: `segments`: document numbers never fall along the context; each of the 4 documents covers 1 to 768 positions, and one covers exactly 768.
All inputs are finite; a program needn't handle non-finite values.
Results may differ from a plain program's by a relative error of at most 0.03.
Values may be sent and summed in bfloat16 or wider, within the bound.
No kernel may reach another device: no remote copies, remote signals or barrier semaphores. Data moves between devices by JAX's collectives and lax.ppermute only.
A program may use at most 192 MiB of HBM per device.

v0:
```python
import math
import jax
import jax.numpy as jnp
from jax import lax
from jax.sharding import PartitionSpec as P

HD = 128
D = 4096
KS = 7
KM = 128
epsilon = 1e-06


def as_sent(shard):

    def short(part):
        return part.astype(jnp.bfloat16) if part.dtype == jnp.float32 else part

    return jax.tree.map(short, shard)


def passed_along(value, axis, steps):
    count = lax.axis_size(axis)
    leading, last = (max(0, -steps), min(count, count - steps))
    return lax.ppermute(value, axis, [(source, source + steps) for source in range(leading, last)])


def depthwise(padded, tap_rows):
    return lax.conv_general_dilated(
        padded[None],
        tap_rows[:, None, :],
        (1,),
        "VALID",
        dimension_numbers=("NWC", "WIO", "NWC"),
        feature_group_count=padded.shape[1],
        precision=lax.Precision.HIGHEST,
    )[0]


def neighbor_rows(edge_rows, offset):
    return passed_along(as_sent(edge_rows), "ctx", offset).astype(edge_rows.dtype)


def channel_total(partial_value):
    return lax.psum(partial_value, "tp")


def shards(
    stream,
    shutter,
    feeder,
    stencil,
    valves,
    intake,
    kernel,
    scaling,
    queries,
    matchers,
    segments,
    cotangent,
):
    local_rows = stream.shape[0]
    width_local = stream.shape[1]
    head_count = width_local // HD
    total_rows = local_rows * lax.axis_size("ctx")
    position = lax.axis_index("ctx") * local_rows
    scale_factor = 1.0 / math.sqrt(HD)
    widened = stream.astype(jnp.float32)
    inner_one = feeder.astype(jnp.float32) * widened
    rim_one = neighbor_rows(inner_one[local_rows - (KS - 1) :], 1)
    padded_one = jnp.concatenate([rim_one, inner_one], axis=0)
    conv_one = depthwise(padded_one, stencil[::-1])
    first_out = (widened + shutter.astype(jnp.float32) * conv_one).astype(jnp.bfloat16)
    first_wide = first_out.astype(jnp.float32)
    inner_two = intake.astype(jnp.float32) * first_wide
    rim_two = neighbor_rows(inner_two[local_rows - (KM - 1) :], 1)
    padded_two = jnp.concatenate([rim_two, inner_two], axis=0)
    conv_two = depthwise(padded_two, kernel[::-1])
    second_out = (first_wide + valves.astype(jnp.float32) * conv_two).astype(jnp.bfloat16)
    second_wide = second_out.astype(jnp.float32)
    squares = channel_total(jnp.sum(second_wide * second_wide, axis=1))
    inverse_rms = lax.rsqrt(squares / D + epsilon)
    normed = (second_wide * inverse_rms[:, None] * scaling).astype(jnp.bfloat16)
    keys_whole, values_whole = (
        lax.all_gather(matchers, "ctx", axis=0, tiled=True),
        lax.all_gather(normed, "ctx", axis=0, tiled=True),
    )
    query_pos = position + jnp.arange(local_rows, dtype=jnp.int32)
    key_pos = jnp.arange(total_rows, dtype=jnp.int32)
    query_seg = lax.dynamic_slice_in_dim(segments, position, local_rows, 0)
    visible = (key_pos[None, :] <= query_pos[:, None]) & (segments[None, :] == query_seg[:, None])
    contract = (((1,), (1,)), ((), ()))
    weight_list = []
    dscore_list = []
    attended_list = []
    query_grad_list = []
    logsum_list = []
    delta_list = []
    for head_index in range(head_count):
        columns = slice(head_index * HD, (head_index + 1) * HD)
        query_head = queries[:, columns]
        key_head = keys_whole[:, columns]
        value_head = values_whole[:, columns]
        cotangent_head = cotangent[:, columns]
        scores = (
            lax.dot_general(query_head, key_head, contract, preferred_element_type=jnp.float32)
            * scale_factor
        )
        scores = jnp.where(visible, scores, -jnp.inf)
        row_max = jnp.max(scores, axis=1)
        logsum = row_max + jnp.log(jnp.sum(jnp.exp(scores - row_max[:, None]), axis=1))
        weights = jnp.exp(scores - logsum[:, None]).astype(jnp.bfloat16)
        attended = jnp.dot(weights, value_head, preferred_element_type=jnp.float32)
        weight_grad = lax.dot_general(
            cotangent_head, value_head, contract, preferred_element_type=jnp.float32
        )
        row_delta = jnp.sum(cotangent_head.astype(jnp.float32) * attended, axis=1)
        dscore = (
            scale_factor * weights.astype(jnp.float32) * (weight_grad - row_delta[:, None])
        ).astype(jnp.bfloat16)
        query_grad = jnp.dot(dscore, key_head, preferred_element_type=jnp.float32)
        weight_list.append(weights)
        dscore_list.append(dscore)
        attended_list.append(attended)
        query_grad_list.append(query_grad)
        logsum_list.append(logsum)
        delta_list.append(row_delta)
    attended_all = jnp.concatenate(attended_list, axis=1)
    result = (second_wide + attended_all).astype(jnp.bfloat16)
    queries_grad = jnp.concatenate(query_grad_list, axis=1).astype(jnp.bfloat16)
    query_heads = queries.reshape(local_rows, head_count, HD)
    cotangent_heads = cotangent.reshape(local_rows, head_count, HD)
    weights_all = jnp.stack(weight_list)
    dscore_all = jnp.stack(dscore_list)
    dscore_part = lax.slice_in_dim(dscore_all, 0, local_rows * lax.axis_size("ctx"), axis=2)
    key_part = jnp.einsum(
        "hts,the->she", dscore_part, query_heads, preferred_element_type=jnp.float32
    )
    value_part = jnp.einsum(
        "hts,the->she", weights_all, cotangent_heads, preferred_element_type=jnp.float32
    )
    summed = lax.psum_scatter(
        jnp.concatenate(
            [
                key_part.reshape(local_rows * lax.axis_size("ctx"), width_local),
                value_part.reshape(local_rows * lax.axis_size("ctx"), width_local),
            ],
            axis=1,
        ).astype(jnp.bfloat16),
        "ctx",
        scatter_dimension=0,
        tiled=True,
    ).astype(jnp.float32)
    matchers_grad = summed[:, :width_local].astype(jnp.bfloat16)
    value_grad = summed[:, width_local:]
    gain_part = value_grad * scaling
    projected = channel_total(jnp.sum(gain_part * second_wide, axis=1))
    scaling_part = jnp.sum(value_grad * second_wide * inverse_rms[:, None], axis=0)
    second_grad = (
        cotangent.astype(jnp.float32)
        + inverse_rms[:, None] * gain_part
        - second_wide * (inverse_rms**3 * projected / D)[:, None]
    )
    valves_grad = (second_grad * conv_two).astype(jnp.bfloat16)
    dconv_two = second_grad * valves.astype(jnp.float32)
    back_two = neighbor_rows(dconv_two[: KM - 1], -1)
    dinner_two = depthwise(jnp.concatenate([dconv_two, back_two], axis=0), kernel)
    intake_grad = (dinner_two * first_wide).astype(jnp.bfloat16)
    kernel_part = depthwise(padded_two, dconv_two)[::-1]
    first_grad = second_grad + dinner_two * intake.astype(jnp.float32)
    shutter_grad = (first_grad * conv_one).astype(jnp.bfloat16)
    dconv_one = first_grad * shutter.astype(jnp.float32)
    back_one = neighbor_rows(dconv_one[: KS - 1], -1)
    dinner_one = depthwise(jnp.concatenate([dconv_one, back_one], axis=0), stencil)
    feeder_grad = (dinner_one * widened).astype(jnp.bfloat16)
    stencil_part = depthwise(padded_one, dconv_one)[::-1]
    stream_grad = (first_grad + dinner_one * feeder.astype(jnp.float32)).astype(jnp.bfloat16)
    stencil_sum, kernel_sum, scaling_sum = (
        lax.psum(stencil_part.astype(jnp.bfloat16), "ctx").astype(jnp.float32),
        lax.psum(kernel_part.astype(jnp.bfloat16), "ctx").astype(jnp.float32),
        lax.psum(scaling_part.astype(jnp.bfloat16), "ctx").astype(jnp.float32),
    )
    normalizer = math.sqrt(total_rows)
    return (
        result,
        stream_grad,
        shutter_grad,
        feeder_grad,
        stencil_sum / normalizer,
        valves_grad,
        intake_grad,
        kernel_sum / normalizer,
        scaling_sum / normalizer,
        queries_grad,
        matchers_grad,
    )


def solution(mesh):
    placed = (
        P("ctx", "tp"),
        P("ctx", "tp"),
        P("ctx", "tp"),
        P(None, "tp"),
        P("ctx", "tp"),
        P("ctx", "tp"),
        P(None, "tp"),
        P("tp"),
        P("ctx", "tp"),
        P("ctx", "tp"),
        P(),
        P("ctx", "tp"),
    )
    return jax.shard_map(
        shards,
        mesh=mesh,
        in_specs=placed,
        out_specs=(
            P("ctx", "tp"),
            P("ctx", "tp"),
            P("ctx", "tp"),
            P("ctx", "tp"),
            P(None, "tp"),
            P("ctx", "tp"),
            P("ctx", "tp"),
            P(None, "tp"),
            P("tp"),
            P("ctx", "tp"),
            P("ctx", "tp"),
        ),
        check_vma=False,
    )
```

profile of v0, /device:TPU:0, one launch (start us, length us, event | category | flops | bytes accessed | tf_op | source)
XLA Modules:
  0.0 272.9 jit_solution(10646670163490515569)
XLA Ops:
  9.1 2.4 collective-permute-start
  11.4 2.8 %rev.12 = f32[7,1024]{1,0:T(8,128)S(1)} reverse(f32[7,1024]{1,0:T(8,128)} %param.15), dimensions={0} | reverse | bytes 57344 | tf_op jit(solution)/shard_map/rev | solution.py:72
  18.3 4.5 %collective-permute-start.1 = (bf16[127,1024]{1,0:T(8,128)(2,1)}, bf16[127,1024]{1,0:T(8,128)(2,1)S(1)}, u32[]{:S(2)}, u32[]{:S(2)}) collective-permute-start(bf16[127,1024]{1,0:T(8,128)(2,1)} %slice.349), channel_id=1, source_target_pairs={{0,4},{4,8},{8,12},{12,16},{16,20},{20,24},{24,28},{1,5},{5,9},{9,... | collective-permute-start | bytes 780296 | tf_op jit(solution)/shard_map/ppermute | solution.py:25
  25.1 5.6 %fusion.74 = f32[1,128,1024]{2,0,1:T(1,128)S(1)} fusion(f32[1,255,1024]{2,0,1:T(1,128)S(1)} %broadcast_in_dim.33, f32[128,1,1024]{2,0,1:T(8,128)S(1)} %bitcast.165), kind=kOutput, calls=%fused_computation.133 | convolution fusion | flops 201326592 | bytes 2093056 | tf_op jit(solution)/shard_map/conv_general_dilated | solution.py:29
  31.6 11.9 %psum.35 = f32[128]{0:T(128)S(1)} all-reduce(f32[128]{0:T(128)S(1)} %get-tuple-element.63), channel_id=1, replica_groups=mesh['ctx'=8,'tp'=4] {'tp'}, use_global_device_ids=true, to_apply=%region_3.4 | all-reduce | flops 128 | bytes 1024 | tf_op jit(solution)/shard_map/psum | solution.py:45
  44.7 1.3 fusion.150
  46.2 1.3 fusion.151
  47.8 1.3 fusion.152
  49.3 1.3 fusion.153
  50.9 1.3 fusion.154
  52.5 1.3 fusion.155
  54.0 1.3 fusion.156
  55.6 1.3 fusion.157
  64.7 2.6 copy.116
  67.3 7.6 %all-gather.5.cloned.1.call-done = bf16[1024,1024]{1,0:T(8,128)(2,1)} async-done(((bf16[128,1024]{1,0:T(8,128)(2,1)}), bf16[1024,1024]{1,0:T(8,128)(2,1)}) %all-gather.5.cloned.1.call-update) | async-done | bytes 2097168 | tf_op jit(solution)/shard_map/all_gather | solution.py:86
  74.9 1.4 fusion.87
  76.4 1.3 fusion.92
  77.7 1.3 fusion.97
  79.0 1.3 fusion.102
  80.3 1.2 fusion.107
  91.7 2.6 copy.114
  94.3 4.7 %pad_maximum_fusion = bf16[1024,2048]{1,0:T(8,128)(2,1)} fusion(bf16[1024,1024]{1,0:T(8,128)(2,1)} %copy.116, bf16[1024,1024]{1,0:T(8,128)(2,1)} %copy.114), kind=kLoop, calls=%fused_computation | loop fusion | flops 8388608 | bytes 8388608 | tf_op jit(solution)/shard_map/concatenate | solution.py:143
  99.3 1.7 copy.68
  101.0 1.6 copy.67
  104.3 1.5 constant_dynamic-update-slice_fusion.7
  105.8 1.5 constant_dynamic-update-slice_fusion.6
  107.3 1.5 constant_dynamic-update-slice_fusion.5
  108.8 1.5 constant_dynamic-update-slice_fusion.4
  111.6 1.9 fusion.39
  113.5 1.9 fusion.38
  115.4 1.8 fusion.37
  117.2 1.8 fusion.36
  119.1 1.9 fusion.35
  120.9 1.9 fusion.34
  124.7 25.8 %reduce-scatter.2.cloned.1.call-done = bf16[128,2048]{1,0:T(8,128)(2,1)} async-done(((bf16[1024,2048]{1,0:T(8,128)(2,1)}), bf16[128,2048]{1,0:T(8,128)(2,1)}) %reduce-scatter.2.cloned.1.call-update) | async-done | bytes 524304 | tf_op jit(solution)/shard_map/reduce_scatter | solution.py:142
  151.7 11.7 %psum.36 = f32[128]{0:T(128)S(1)} all-reduce(f32[128]{0:T(128)S(1)} %get-tuple-element.34), channel_id=1, replica_groups=mesh['ctx'=8,'tp'=4] {'tp'}, use_global_device_ids=true, to_apply=%region_28.29 | all-reduce | flops 128 | bytes 1024 | tf_op jit(solution)/shard_map/psum | solution.py:45
  163.4 1.2 convert_multiply_fusion.11
  164.6 6.8 %fusion.70 = bf16[1,128,1024]{2,0,1:T(2,128)(2,1)S(1)} fusion(f32[1,255,1024]{2,0,1:T(1,128)} %copy-done.30, f32[128,1,1024]{2,0,1:T(8,128)S(1)} %bitcast.159), kind=kOutput, calls=%fused_computation.129 | convolution fusion | flops 201326592 | bytes 1830912 | tf_op jit(solution)/shard_map/conv_general_dilated | solution.py:29
  171.5 2.6 rev.15
  174.9 1.3 collective-permute-start.2
  176.9 1.8 copy.104
  179.4 45.7 %all-reduce.3.cloned.1.call-done = bf16[128,1024]{1,0:T(8,128)(2,1)} async-done(((bf16[128,1024]{1,0:T(8,128)(2,1)}), bf16[128,1024]{1,0:T(8,128)(2,1)}) %all-reduce.3.cloned.1.call-update) | async-done | bytes 262160 | tf_op jit(solution)/shard_map/psum | solution.py:180
  225.1 1.8 convert_multiply_fusion.16
  227.1 5.8 %fusion.40 = f32[1,128,1024]{2,0,1:T(1,128)S(1)} fusion(f32[1,255,1024]{2,1,0:T(8,128)S(1)} %maximum_bitcast_fusion, f32[128,1,1024]{2,0,1:T(8,128)S(1)} %bitcast.164), kind=kOutput, calls=%fused_computation.77 | convolution fusion | flops 201326592 | bytes 2093056 | tf_op jit(solution)/shard_map/conv_general_dilated | solution.py:29
  232.9 2.7 %multiply_convert_fusion = (bf16[128,1024]{1,0:T(8,128)(2,1)}, f32[128,1024]{1,0:T(8,128)S(1)}, bf16[128,1024]{1,0:T(8,128)(2,1)}, bf16[128,1024]{1,0:T(8,128)(2,1)}, bf16[128,1024]{1,0:T(8,128)(2,1)}) fusion(f32[1,136,1024]{2,1,0:T(8,128)S(1)} %reshape.119, bf16[128,1024]{1,0:T(8,128)(2,1)S(1)} %copy-done.26, f32[1,128,1024]{2,0,1:T(1,128)S(1)} %fusion.40, ...), kind=kLoop, calls=%fused_computation.136 | loop fusion | flops 2621440 | bytes 4985856 | tf_op jit(solution)/shard_map/convert_element_type | solution.py:171
  237.1 22.4 %all-reduce = (bf16[7,1024]{1,0:T(8,128)(2,1)S(1)}, bf16[1024]{0:T(1024)(128)(2,1)S(1)}) all-reduce(bf16[7,1024]{1,0:T(8,128)(2,1)S(1)} %rev.14, bf16[1024]{0:T(1024)(128)(2,1)S(1)} %get-tuple-element.33), channel_id=1, replica_groups=mesh['ctx'=8,'tp'=4] {'ctx'}, use_global_device_ids=true, to_apply=%region_29.30 | all-reduce | flops 8192 | bytes 32768 | tf_op jit(solution)/shard_map/psum | solution.py:179
  260.1 1.3 collective-permute-start.3
  262.0 1.2 collective-permute-done.3
  (191 shorter events, 43.8 us)
Async XLA Ops:
  7.2 37.5 %all-gather.3.cloned.1.call-start = ((), (), s32[]{:S(2)}) async-start(), calls=%async_computation.1 | async-start | bytes 2359296 | tf_op jit(solution)/shard_map/all_gather | solution.py:85
  7.9 67.0 %all-gather.5.cloned.1.call-start = ((), (), s32[]{:S(2)}) async-start(), calls=%async_computation.2 | async-start | bytes 2359296 | tf_op jit(solution)/shard_map/all_gather | solution.py:86
  9.1 5.2 %collective-permute-start = (bf16[6,1024]{1,0:T(8,128)(2,1)S(1)}, bf16[6,1024]{1,0:T(8,128)(2,1)S(1)}, u32[]{:S(2)}, u32[]{:S(2)}) collective-permute-start(bf16[6,1024]{1,0:T(8,128)(2,1)S(1)} %slice.351), channel_id=1, source_target_pairs={{0,4},{4,8},{8,12},{12,16},{16,20},{20,24},{24,28},{1,5},{5,9},{9,... | collective-permute-start | bytes 36872 | tf_op jit(solution)/shard_map/ppermute | solution.py:25
  15.1 0.9 copy-start.40
  16.2 1.0 copy-start.11
  16.3 1.0 copy-start.25
  16.3 1.1 copy-start.27
  16.6 6.2 %copy-start.33 = (f32[128,1024]{1,0:T(8,128)S(1)}, f32[128,1024]{1,0:T(8,128)}, u32[]{:S(2)}) copy-start(f32[128,1024]{1,0:T(8,128)} %param.18) | copy-start | bytes 1572868
  17.4 5.8 %copy-start.1 = (bf16[128,1024]{1,0:T(8,128)(2,1)S(1)}, bf16[128,1024]{1,0:T(8,128)(2,1)}, u32[]{:S(2)}) copy-start(bf16[128,1024]{1,0:T(8,128)(2,1)} %param.23) | copy-start | bytes 786436
  17.4 5.9 %copy-start.36 = (bf16[128,1024]{1,0:T(8,128)(2,1)S(1)}, bf16[128,1024]{1,0:T(8,128)(2,1)}, u32[]{:S(2)}) copy-start(bf16[128,1024]{1,0:T(8,128)(2,1)} %param.20) | copy-start | bytes 786436
  17.4 6.8 %copy-start.39 = (s32[1024]{0:T(1024)S(1)}, s32[1024]{0:T(1024)}, u32[]{:S(2)}) copy-start(s32[1024]{0:T(1024)} %param.22) | copy-start | bytes 12292
  17.5 13.3 %copy-start.2 = (bf16[128,1024]{1,0:T(8,128)(2,1)}, bf16[128,1024]{1,0:T(8,128)(2,1)S(1)}, u32[]{:S(2)}) copy-start(bf16[128,1024]{1,0:T(8,128)(2,1)S(1)} %get-tuple-element.66) | copy-start | bytes 786436
  18.3 5.9 %collective-permute-start.1 = (bf16[127,1024]{1,0:T(8,128)(2,1)}, bf16[127,1024]{1,0:T(8,128)(2,1)S(1)}, u32[]{:S(2)}, u32[]{:S(2)}) collective-permute-start(bf16[127,1024]{1,0:T(8,128)(2,1)} %slice.349), channel_id=1, source_target_pairs={{0,4},{4,8},{8,12},{12,16},{16,20},{20,24},{24,28},{1,5},{5,9},{9,... | collective-permute-start | bytes 780296 | tf_op jit(solution)/shard_map/ppermute | solution.py:25
  25.1 5.7 %copy-start.30 = (f32[1,255,1024]{2,0,1:T(1,128)}, f32[1,255,1024]{2,0,1:T(1,128)S(1)}, u32[]{:S(2)}) copy-start(f32[1,255,1024]{2,0,1:T(1,128)S(1)} %broadcast_in_dim.33) | copy-start | bytes 3133444
  25.1 5.7 %copy-start.20 = (bf16[128,1024]{1,0:T(8,128)(2,1)S(1)}, bf16[128,1024]{1,0:T(8,128)(2,1)}, u32[]{:S(2)}) copy-start(bf16[128,1024]{1,0:T(8,128)(2,1)} %param.16) | copy-start | bytes 786436
  25.1 18.4 %copy-start.37 = (f32[1024]{0:T(1024)S(1)}, f32[1024]{0:T(1024)}, u32[]{:S(2)}) copy-start(f32[1024]{0:T(1024)} %param.19) | copy-start | bytes 12292
  30.8 0.8 copy-start.15
  44.4 106.1 %reduce-scatter.2.cloned.1.call-start = ((), (), s32[]{:S(2)}) async-start(), calls=%async_computation.3 | async-start | bytes 4718592 | tf_op jit(solution)/shard_map/reduce_scatter | solution.py:142
  67.3 14.2 %copy-start.4 = (bf16[128,1024]{1,0:T(8,128)(2,1)S(1)}, bf16[128,1024]{1,0:T(8,128)(2,1)}, u32[]{:S(2)}) copy-start(bf16[128,1024]{1,0:T(8,128)(2,1)} %get-tuple-element.60) | copy-start | bytes 786436
  74.9 5.4 %copy-start = (bf16[1024,1024]{1,0:T(8,128)(2,1)S(1)}, bf16[1024,1024]{1,0:T(8,128)(2,1)}, u32[]{:S(2)}) copy-start(bf16[1024,1024]{1,0:T(8,128)(2,1)} %all-gather.5.cloned.1.call-done) | copy-start | bytes 6291460
  74.9 6.9 %copy-start.24 = (bf16[128,1024]{1,0:T(8,128)(2,1)S(1)}, bf16[128,1024]{1,0:T(8,128)(2,1)}, u32[]{:S(2)}) copy-start(bf16[128,1024]{1,0:T(8,128)(2,1)} %get-tuple-element.62) | copy-start | bytes 786436
  74.9 7.3 %copy-start.10 = (bf16[128,1024]{1,0:T(8,128)(2,1)S(1)}, bf16[128,1024]{1,0:T(8,128)(2,1)}, u32[]{:S(2)}) copy-start(bf16[128,1024]{1,0:T(8,128)(2,1)} %get-tuple-element.48) | copy-start | bytes 786436
  81.8 1.3 copy-start.31
  81.8 3.2 %copy-start.5 = (bf16[128,1024]{1,0:T(8,128)(2,1)S(1)}, bf16[128,1024]{1,0:T(8,128)(2,1)}, u32[]{:S(2)}) copy-start(bf16[128,1024]{1,0:T(8,128)(2,1)} %get-tuple-element.58) | copy-start | bytes 786436
  82.2 1.0 copy-start.32
  82.2 3.9 %copy-start.6 = (bf16[128,1024]{1,0:T(8,128)(2,1)S(1)}, bf16[128,1024]{1,0:T(8,128)(2,1)}, u32[]{:S(2)}) copy-start(bf16[128,1024]{1,0:T(8,128)(2,1)} %get-tuple-element.56) | copy-start | bytes 786436
  83.1 3.9 %copy-start.7 = (bf16[128,1024]{1,0:T(8,128)(2,1)S(1)}, bf16[128,1024]{1,0:T(8,128)(2,1)}, u32[]{:S(2)}) copy-start(bf16[128,1024]{1,0:T(8,128)(2,1)} %get-tuple-element.54) | copy-start | bytes 786436
  84.1 3.9 %copy-start.8 = (bf16[128,1024]{1,0:T(8,128)(2,1)S(1)}, bf16[128,1024]{1,0:T(8,128)(2,1)}, u32[]{:S(2)}) copy-start(bf16[128,1024]{1,0:T(8,128)(2,1)} %get-tuple-element.52) | copy-start | bytes 786436
  85.1 3.9 %copy-start.9 = (bf16[128,1024]{1,0:T(8,128)(2,1)S(1)}, bf16[128,1024]{1,0:T(8,128)(2,1)}, u32[]{:S(2)}) copy-start(bf16[128,1024]{1,0:T(8,128)(2,1)} %get-tuple-element.50) | copy-start | bytes 786436
  87.0 3.9 %copy-start.19 = (bf16[128,1024]{0,1:T(8,128)(2,1)S(1)}, bf16[128,1024]{0,1:T(8,128)(2,1)}, u32[]{:S(2)}) copy-start(bf16[128,1024]{0,1:T(8,128)(2,1)} %copy.113) | copy-start | bytes 786436
  99.0 12.6 %copy-start.17 = (bf16[1024,1024]{1,0:T(8,128)(2,1)S(1)}, bf16[1024,1024]{1,0:T(8,128)(2,1)}, u32[]{:S(2)}) copy-start(bf16[1024,1024]{1,0:T(8,128)(2,1)} %all-gather.3.cloned.1.call-done) | copy-start | bytes 6291460
  99.0 126.1 %all-reduce.3.cloned.1.call-start = ((), (), s32[]{:S(2)}) async-start(), calls=%async_computation.4 | async-start | bytes 524288 | tf_op jit(solution)/shard_map/psum | solution.py:180
  104.3 18.6 %copy-start.22 = (bf16[128,1024]{1,0:T(8,128)(2,1)S(1)}, bf16[128,1024]{1,0:T(8,128)(2,1)}, u32[]{:S(2)}) copy-start(bf16[128,1024]{1,0:T(8,128)(2,1)} %get-tuple-element.102) | copy-start | bytes 786436
  110.3 13.4 %copy-start.23 = (bf16[128,1024]{1,0:T(8,128)(2,1)S(1)}, bf16[128,1024]{1,0:T(8,128)(2,1)}, u32[]{:S(2)}) copy-start(bf16[128,1024]{1,0:T(8,128)(2,1)} %get-tuple-element.104) | copy-start | bytes 786436
  113.5 49.9 %copy-start.21 = (bf16[128,1024]{1,0:T(8,128)(2,1)S(1)}, bf16[128,1024]{1,0:T(8,128)(2,1)}, u32[]{:S(2)}) copy-start(bf16[128,1024]{1,0:T(8,128)(2,1)} %param.16) | copy-start | bytes 786436
  164.6 10.2 %copy-start.35 = (f32[128,128]{0,1:T(8,128)S(1)}, f32[128,128]{0,1:T(8,128)}, u32[]{:S(2)}) copy-start(f32[128,128]{0,1:T(8,128)} %get-tuple-element.88) | copy-start | bytes 196612
  171.4 7.2 %copy-start.18 = (bf16[128,2048]{1,0:T(8,128)(2,1)S(1)}, bf16[128,2048]{1,0:T(8,128)(2,1)}, u32[]{:S(2)}) copy-start(bf16[128,2048]{1,0:T(8,128)(2,1)} %reduce-scatter.2.cloned.1.call-done) | copy-start | bytes 1572868
  174.9 51.9 %collective-permute-start.2 = (bf16[127,1024]{1,0:T(8,128)(2,1)S(1)}, bf16[127,1024]{1,0:T(8,128)(2,1)S(1)}, u32[]{:S(2)}, u32[]{:S(2)}) collective-permute-start(bf16[127,1024]{1,0:T(8,128)(2,1)S(1)} %slice.348), channel_id=1, source_target_pairs={{4,0},{8,4},{12,8},{16,12},{20,16},{24,20},{28,24},{5,1},{9,5},{13... | collective-permute-start | bytes 780296 | tf_op jit(solution)/shard_map/ppermute | solution.py:25
  178.7 48.4 %copy-start.34 = (f32[128,1024]{1,0:T(8,128)S(1)}, f32[128,1024]{1,0:T(8,128)}, u32[]{:S(2)}) copy-start(f32[128,1024]{1,0:T(8,128)} %param.18) | copy-start | bytes 1572868
  227.0 5.8 %copy-start.3 = (bf16[128,1024]{1,0:T(8,128)(2,1)S(1)}, bf16[128,1024]{1,0:T(8,128)(2,1)}, u32[]{:S(2)}) copy-start(bf16[128,1024]{1,0:T(8,128)(2,1)} %copy-done.2) | copy-start | bytes 786436
  227.1 5.8 %copy-start.16 = (f32[1,128,1024]{2,0,1:T(1,128)S(1)}, f32[1,128,1024]{2,0,1:T(1,128)}, u32[]{:S(2)}) copy-start(f32[1,128,1024]{2,0,1:T(1,128)} %copy-done.15) | copy-start | bytes 1572868
  227.1 5.8 %copy-start.26 = (bf16[128,1024]{1,0:T(8,128)(2,1)S(1)}, bf16[128,1024]{1,0:T(8,128)(2,1)}, u32[]{:S(2)}) copy-start(bf16[128,1024]{1,0:T(8,128)(2,1)} %param.17) | copy-start | bytes 786436
  232.9 2.8 %copy-start.28 = (bf16[128,1024]{1,0:T(8,128)(2,1)S(1)}, bf16[128,1024]{1,0:T(8,128)(2,1)}, u32[]{:S(2)}) copy-start(bf16[128,1024]{1,0:T(8,128)(2,1)} %param.13) | copy-start | bytes 786436
  232.9 2.8 %copy-start.14 = (f32[1,134,1024]{2,1,0:T(8,128)S(1)}, f32[1,134,1024]{2,1,0:T(8,128)}, u32[]{:S(2)}) copy-start(f32[1,134,1024]{2,1,0:T(8,128)} %copy-done.13) | copy-start | bytes 1646596
  260.1 3.1 %collective-permute-start.3 = (bf16[6,1024]{1,0:T(8,128)(2,1)S(1)}, bf16[6,1024]{1,0:T(8,128)(2,1)S(1)}, u32[]{:S(2)}, u32[]{:S(2)}) collective-permute-start(bf16[6,1024]{1,0:T(8,128)(2,1)S(1)} %slice.350), channel_id=1, source_target_pairs={{4,0},{8,4},{12,8},{16,12},{20,16},{24,20},{28,24},{5,1},{9,5},{13... | collective-permute-start | bytes 36872 | tf_op jit(solution)/shard_map/ppermute | solution.py:25
  263.2 0.9 copy-start.38
  264.4 1.0 copy-start.12
  264.4 1.0 copy-start.29
  (1 other events, 0.8 us)
Sparse Core Ops, SparseCore 0:
  9.9 30.5 all-gather.2
  44.5 30.3 all-gather.4
  99.1 51.3 reduce-scatter.1
  174.3 50.7 all-reduce.2
where the time goes:
time: 274 us; the launch traced here: 273 us
  waiting for transfers between devices  81 us (30%)
  matrix products  60.8 us (22%)
  blocking collectives  46 us (17%)
  local copies, waits for them, and re-layouts  35.2 us (13%)
  other arithmetic  25.2 us (9%)
  between operations  14.6 us (5%)
  starting transfers between devices  10 us (4%)
    psum x1, waiting for transfers between devices, shards(): lax.psum(kernel_part.astype(jnp.bfloat16), 'ctx').astype(jnp.float32)  45.7 us
    reduce_scatter x1, waiting for transfers between devices, shards(): lax.psum_scatter(jnp.concatenate([key_part.reshape(local_rows * lax.axis_...  25.8 us
    psum x2, blocking collectives, channel_total(): return lax.psum(partial_value, 'tp')  23.6 us
    psum x1, blocking collectives, shards(): lax.psum(stencil_part.astype(jnp.bfloat16), 'ctx').astype(jnp.float32)  22.4 us
    conv_general_dilated x6, matrix products, depthwise(): lax.conv_general_dilated(padded[None], tap_rows[:, None, :], (1,), 'VALID...  19.9 us
    dot_general x8, matrix products, shards(): query_grad = jnp.dot(dscore, key_head, preferred_element_type=jnp.float32)  13 us
    unnamed x93, local copies, waits for them, and re-layouts  12.7 us
    dot_general x8, matrix products, shards(): lax.dot_general(query_head, key_head, contract, preferred_element_type=jn...  10.6 us
  transfers between devices with their start and end apart: 8, of which 4 were waited for; matrix products, arithmetic and copies ran while one was open for 25% of the time, Pallas kernels for 0%

commit v1 on v0

--- a/solution.py
+++ b/solution.py
@@ -1,14 +1,35 @@
+import functools
 import math
 import jax
 import jax.numpy as jnp
 from jax import lax
 from jax.sharding import PartitionSpec as P
+from jax.lax import axis_index, axis_size, ppermute
 
 HD = 128
 D = 4096
 KS = 7
 KM = 128
 epsilon = 1e-06
+
+
+def touch_shards(my_data, comm_axis, ndim_at):
+    parts_n = axis_size(comm_axis)
+    sides = tuple(((dev_i, (dev_i + 1) % parts_n) for dev_i in range(parts_n)))
+    b_now, built = ([my_data], [my_data])
+    by_rank = tuple(((dev_i, (dev_i - 1) % parts_n) for dev_i in range(parts_n)))
+    for _ in range(parts_n // 2):
+        b_now.append(ppermute(b_now[-1], axis_name=comm_axis, perm=sides))
+    for _ in range((parts_n - 1) // 2):
+        built.append(ppermute(built[-1], axis_name=comm_axis, perm=by_rank))
+    v1 = jnp.concatenate([*b_now[::-1], *built[1:]], axis=ndim_at)
+    m_next = jnp.roll(
+        v1, (axis_index(comm_axis) - parts_n // 2) * my_data.shape[ndim_at], axis=ndim_at
+    )
+    return m_next
+
+
+set_sums_all = functools.partial(touch_shards, comm_axis="ctx", ndim_at=0)
 
 
 def as_sent(shard):
@@ -83,7 +104,7 @@
     normed = (second_wide * inverse_rms[:, None] * scaling).astype(jnp.bfloat16)
     keys_whole, values_whole = (
         lax.all_gather(matchers, "ctx", axis=0, tiled=True),
-        lax.all_gather(normed, "ctx", axis=0, tiled=True),
+        set_sums_all(normed),
     )
     query_pos = position + jnp.arange(local_rows, dtype=jnp.int32)
     key_pos = jnp.arange(total_rows, dtype=jnp.int32)

time: 274 us -> 320 us (1.17)
  local copies, waits for them, and re-layouts: 35.2 us -> 51.9 us
  waiting for transfers between devices: 81 us -> 97.6 us
  starting transfers between devices: 10 us -> 18.3 us
  matrix products: 60.8 us -> 69 us
  other arithmetic: 25.2 us -> 20.6 us
    ppermute x0 -> x7, waiting for transfers between devices: none -> 27.8 us  [the longest x4 27.8 us: touch_shards(): b_now.append(ppermute(b_now[-1], axis_name=comm_axis, perm=sides))]
    unnamed x93 -> x106, local copies, waits for them, and re-layouts: 12.7 us -> 23.3 us
    ppermute x0 -> x7, starting transfers between devices: none -> 8.51 us  [the longest x3 8.12 us: touch_shards(): built.append(ppermute(built[-1], axis_name=comm_axis, perm=by_rank))]
    dot_general x8, matrix products: 7.84 us -> 15.4 us  [shards(): lax.dot_general(cotangent_head, value_head, contract, preferred_element_t...]
    all_gather x1 -> x0, waiting for transfers between devices: 7.58 us -> none  [shards(): lax.all_gather(normed, 'ctx', axis=0, tiled=True)]
    dot_general x8, local copies, waits for them, and re-layouts: 5.06 us -> 10.3 us  [shards(): attended = jnp.dot(weights, value_head, preferred_element_type=jnp.float32)]
    dot_general x8, matrix products: 13 us -> 9.17 us  [shards(): query_grad = jnp.dot(dscore, key_head, preferred_element_type=jnp.float32)]
    reduce_scatter x1, waiting for transfers between devices: 25.8 us -> 22.1 us  [shards(): lax.psum_scatter(jnp.concatenate([key_part.reshape(local_rows * lax.axis_...]
  transfers between devices with their start and end apart: 8 -> 14, of which waited for: 4 -> 8; matrix products, arithmetic and copies ran while one was open for 25% -> 18% of each run, Pallas kernels for 0% -> 0%
where the time goes in v1:
time: 320 us; the launch traced here: 318 us
  waiting for transfers between devices  97.6 us (30%)
  matrix products  69 us (22%)
  local copies, waits for them, and re-layouts  51.9 us (16%)
  blocking collectives  46.1 us (14%)
  other arithmetic  20.6 us (6%)
  starting transfers between devices  18.3 us (6%)
  between operations  14.7 us (5%)
    psum x1, waiting for transfers between devices, shards(): lax.psum(kernel_part.astype(jnp.bfloat16), 'ctx').astype(jnp.float32)  45.7 us
    ppermute x4, waiting for transfers between devices, touch_shards(): b_now.append(ppermute(b_now[-1], axis_name=comm_axis, perm=sides))  27.8 us
    psum x2, blocking collectives, channel_total(): return lax.psum(partial_value, 'tp')  23.8 us
    unnamed x106, local copies, waits for them, and re-layouts  23.3 us
    psum x1, blocking collectives, shards(): lax.psum(stencil_part.astype(jnp.bfloat16), 'ctx').astype(jnp.float32)  22.4 us
    reduce_scatter x1, waiting for transfers between devices, shards(): lax.psum_scatter(jnp.concatenate([key_part.reshape(local_rows * lax.axis_...  22.1 us
    conv_general_dilated x6, matrix products, depthwise(): lax.conv_general_dilated(padded[None], tap_rows[:, None, :], (1,), 'VALID...  19.9 us
    dot_general x8, matrix products, shards(): lax.dot_general(cotangent_head, value_head, contract, preferred_element_t...  15.4 us
  transfers between devices with their start and end apart: 14, of which 8 were waited for; matrix products, arithmetic and copies ran while one was open for 18% of the time, Pallas kernels for 0%

profile of v1, /device:TPU:0, one launch (start us, length us, event | category | flops | bytes accessed | tf_op | source)
XLA Modules:
  0.0 318.1 jit_solution(17302481788615317203)
XLA Ops:
  8.3 2.4 collective-permute-start
  10.7 2.8 rev.12
  16.8 4.5 %collective-permute-start.1 = (bf16[127,1024]{1,0:T(8,128)(2,1)S(1)}, bf16[127,1024]{1,0:T(8,128)(2,1)S(1)}, u32[]{:S(2)}, u32[]{:S(2)}) collective-permute-start(bf16[127,1024]{1,0:T(8,128)(2,1)S(1)} %slice.309), channel_id=1, source_target_pairs={{0,4},{4,8},{8,12},{12,16},{16,20},{20,24},{24,28},{1,5},{5,9},{9,... | collective-permute-start | bytes 780296 | tf_op jit(solution)/shard_map/ppermute | solution.py:46
  23.4 5.6 %fusion.74 = f32[1,128,1024]{2,0,1:T(1,128)S(1)} fusion(f32[1,255,1024]{2,0,1:T(1,128)S(1)} %broadcast_in_dim.33, f32[128,1,1024]{2,0,1:T(8,128)S(1)} %bitcast.165), kind=kOutput, calls=%fused_computation.133 | convolution fusion | flops 201326592 | bytes 2093056 | tf_op jit(solution)/shard_map/conv_general_dilated | solution.py:50
  29.3 12.1 %psum.35 = f32[128]{0:T(128)S(1)} all-reduce(f32[128]{0:T(128)S(1)} %get-tuple-element.63), channel_id=1, replica_groups=mesh['ctx'=8,'tp'=4] {'tp'}, use_global_device_ids=true, to_apply=%region_3.4 | all-reduce | flops 128 | bytes 1024 | tf_op jit(solution)/shard_map/psum | solution.py:66
  41.9 10.8 %collective-permute-done.2 = bf16[128,1024]{1,0:T(8,128)(2,1)S(1)} collective-permute-done((bf16[128,1024]{1,0:T(8,128)(2,1)S(1)}, bf16[128,1024]{1,0:T(8,128)(2,1)S(1)}, u32[]{:S(2)}, u32[]{:S(2)}) %collective-permute-start.2) | collective-permute-done | bytes 262176 | tf_op jit(solution)/shard_map/ppermute | solution.py:22
  52.7 2.6 collective-permute-start.6
  55.4 6.8 %collective-permute-done.3 = bf16[128,1024]{1,0:T(8,128)(2,1)S(1)} collective-permute-done((bf16[128,1024]{1,0:T(8,128)(2,1)S(1)}, bf16[128,1024]{1,0:T(8,128)(2,1)S(1)}, u32[]{:S(2)}, u32[]{:S(2)}) %collective-permute-start.3) | collective-permute-done | bytes 262176 | tf_op jit(solution)/shard_map/ppermute | solution.py:22
  62.2 2.6 collective-permute-start.7
  64.8 6.0 %collective-permute-done.4 = bf16[128,1024]{1,0:T(8,128)(2,1)S(1)} collective-permute-done((bf16[128,1024]{1,0:T(8,128)(2,1)S(1)}, bf16[128,1024]{1,0:T(8,128)(2,1)S(1)}, u32[]{:S(2)}, u32[]{:S(2)}) %collective-permute-start.4) | collective-permute-done | bytes 262176 | tf_op jit(solution)/shard_map/ppermute | solution.py:22
  71.0 1.8 copy.113
  72.9 2.8 collective-permute-start.8
  75.7 4.2 %collective-permute-done.5 = bf16[128,1024]{1,0:T(8,128)(2,1)S(1)} collective-permute-done((bf16[128,1024]{1,0:T(8,128)(2,1)S(1)}, bf16[128,1024]{1,0:T(8,128)(2,1)S(1)}, u32[]{:S(2)}, u32[]{:S(2)}) %collective-permute-start.5) | collective-permute-done | bytes 262176 | tf_op jit(solution)/shard_map/ppermute | solution.py:22
  114.5 2.1 multiply_reduce_fusion
  116.6 1.9 bitcast_dynamic-update-slice_fusion.15
  118.5 1.9 bitcast_dynamic-update-slice_fusion.14
  120.5 1.9 bitcast_dynamic-update-slice_fusion.13
  122.4 1.9 bitcast_dynamic-update-slice_fusion.12
  124.3 2.0 bitcast_dynamic-update-slice_fusion.11
  126.3 1.9 bitcast_dynamic-update-slice_fusion.10
  128.2 1.9 bitcast_dynamic-update-slice_fusion.9
  130.1 1.9 bitcast_dynamic-update-slice_fusion.8
  132.8 2.6 copy.114
  135.4 2.3 convolution_convert_fusion
  137.7 2.6 copy.116
  140.3 4.7 %pad_maximum_fusion = bf16[1024,2048]{1,0:T(8,128)(2,1)} fusion(bf16[1024,1024]{1,0:T(8,128)(2,1)} %copy.116, bf16[1024,1024]{1,0:T(8,128)(2,1)} %copy.114), kind=kLoop, calls=%fused_computation | loop fusion | flops 8388608 | bytes 8388608 | tf_op jit(solution)/shard_map/concatenate | solution.py:164
  145.2 1.7 copy.67
  146.9 1.6 copy.68
  148.5 1.6 copy.69
  150.1 1.6 copy.70
  151.6 1.6 copy.71
  153.2 1.6 copy.72
  155.5 1.6 constant_dynamic-update-slice_fusion.23
  157.0 1.5 constant_dynamic-update-slice_fusion.22
  160.0 1.5 constant_dynamic-update-slice_fusion.20
  161.5 1.5 constant_dynamic-update-slice_fusion.19
  165.4 1.9 fusion.38
  167.3 1.8 fusion.37
  173.7 22.1 %reduce-scatter.2.cloned.1.call-done = bf16[128,2048]{1,0:T(8,128)(2,1)} async-done(((bf16[1024,2048]{1,0:T(8,128)(2,1)}), bf16[128,2048]{1,0:T(8,128)(2,1)}) %reduce-scatter.2.cloned.1.call-update) | async-done | bytes 524304 | tf_op jit(solution)/shard_map/reduce_scatter | solution.py:163
  196.9 11.7 %psum.36 = f32[128]{0:T(128)S(1)} all-reduce(f32[128]{0:T(128)S(1)} %get-tuple-element.34), channel_id=1, replica_groups=mesh['ctx'=8,'tp'=4] {'tp'}, use_global_device_ids=true, to_apply=%region_28.29 | all-reduce | flops 128 | bytes 1024 | tf_op jit(solution)/shard_map/psum | solution.py:66
  209.8 6.8 %fusion.70 = bf16[1,128,1024]{2,0,1:T(2,128)(2,1)S(1)} fusion(f32[1,255,1024]{2,0,1:T(1,128)} %copy-done.26, f32[128,1,1024]{2,0,1:T(8,128)S(1)} %bitcast.159), kind=kOutput, calls=%fused_computation.129 | convolution fusion | flops 201326592 | bytes 1830912 | tf_op jit(solution)/shard_map/conv_general_dilated | solution.py:50
  216.8 2.6 rev.15
  222.1 1.8 copy.104
  224.6 45.7 %all-reduce.3.cloned.1.call-done = bf16[128,1024]{1,0:T(8,128)(2,1)} async-done(((bf16[128,1024]{1,0:T(8,128)(2,1)}), bf16[128,1024]{1,0:T(8,128)(2,1)}) %all-reduce.3.cloned.1.call-update) | async-done | bytes 262160 | tf_op jit(solution)/shard_map/psum | solution.py:201
  270.3 1.8 convert_multiply_fusion.16
  272.3 5.8 %fusion.40 = f32[1,128,1024]{2,0,1:T(1,128)S(1)} fusion(f32[1,255,1024]{2,1,0:T(8,128)S(1)} %maximum_bitcast_fusion, f32[128,1,1024]{2,0,1:T(8,128)S(1)} %bitcast.164), kind=kOutput, calls=%fused_computation.77 | convolution fusion | flops 201326592 | bytes 2093056 | tf_op jit(solution)/shard_map/conv_general_dilated | solution.py:50
  278.1 2.7 multiply_convert_fusion
  282.4 22.4 %all-reduce = (bf16[7,1024]{1,0:T(8,128)(2,1)S(1)}, bf16[1024]{0:T(1024)(128)(2,1)S(1)}) all-reduce(bf16[7,1024]{1,0:T(8,128)(2,1)S(1)} %rev.14, bf16[1024]{0:T(1024)(128)(2,1)S(1)} %get-tuple-element.33), channel_id=1, replica_groups=mesh['ctx'=8,'tp'=4] {'ctx'}, use_global_device_ids=true, to_apply=%region_29.30 | all-reduce | flops 8192 | bytes 32768 | tf_op jit(solution)/shard_map/psum | solution.py:200
  (218 shorter events, 66.0 us)
Async XLA Ops:
  7.2 84.6 %all-gather.2.cloned.1.call-start = ((), (), s32[]{:S(2)}) async-start(), calls=%async_computation.1 | async-start | bytes 2359296 | tf_op jit(solution)/shard_map/all_gather | solution.py:106
  8.3 5.2 %collective-permute-start = (bf16[6,1024]{1,0:T(8,128)(2,1)S(1)}, bf16[6,1024]{1,0:T(8,128)(2,1)S(1)}, u32[]{:S(2)}, u32[]{:S(2)}) collective-permute-start(bf16[6,1024]{1,0:T(8,128)(2,1)S(1)} %slice.311), channel_id=1, source_target_pairs={{0,4},{4,8},{8,12},{12,16},{16,20},{20,24},{24,28},{1,5},{5,9},{9,... | collective-permute-start | bytes 36872 | tf_op jit(solution)/shard_map/ppermute | solution.py:46
  15.5 1.1 copy-start.23
  15.9 5.6 %copy-start.33 = (f32[128,1024]{1,0:T(8,128)S(1)}, f32[128,1024]{1,0:T(8,128)}, u32[]{:S(2)}) copy-start(f32[128,1024]{1,0:T(8,128)} %param.18) | copy-start | bytes 1572868
  16.8 12.3 %copy-start.2 = (bf16[128,1024]{1,0:T(8,128)(2,1)}, bf16[128,1024]{1,0:T(8,128)(2,1)S(1)}, u32[]{:S(2)}) copy-start(bf16[128,1024]{1,0:T(8,128)(2,1)S(1)} %get-tuple-element.66) | copy-start | bytes 786436
  16.8 5.7 %collective-permute-start.1 = (bf16[127,1024]{1,0:T(8,128)(2,1)S(1)}, bf16[127,1024]{1,0:T(8,128)(2,1)S(1)}, u32[]{:S(2)}, u32[]{:S(2)}) collective-permute-start(bf16[127,1024]{1,0:T(8,128)(2,1)S(1)} %slice.309), channel_id=1, source_target_pairs={{0,4},{4,8},{8,12},{12,16},{16,20},{20,24},{24,28},{1,5},{5,9},{9,... | collective-permute-start | bytes 780296 | tf_op jit(solution)/shard_map/ppermute | solution.py:46
  21.4 174.3 %reduce-scatter.2.cloned.1.call-start = ((), (), s32[]{:S(2)}) async-start(), calls=%async_computation.2 | async-start | bytes 4718592 | tf_op jit(solution)/shard_map/reduce_scatter | solution.py:163
  23.4 5.7 %copy-start.26 = (f32[1,255,1024]{2,0,1:T(1,128)}, f32[1,255,1024]{2,0,1:T(1,128)S(1)}, u32[]{:S(2)}) copy-start(f32[1,255,1024]{2,0,1:T(1,128)S(1)} %broadcast_in_dim.33) | copy-start | bytes 3133444
  23.4 5.7 %copy-start.19 = (bf16[128,1024]{1,0:T(8,128)(2,1)S(1)}, bf16[128,1024]{1,0:T(8,128)(2,1)}, u32[]{:S(2)}) copy-start(bf16[128,1024]{1,0:T(8,128)(2,1)} %param.16) | copy-start | bytes 786436
  23.4 18.0 %copy-start.37 = (f32[1024]{0:T(1024)S(1)}, f32[1024]{0:T(1024)}, u32[]{:S(2)}) copy-start(f32[1024]{0:T(1024)} %param.19) | copy-start | bytes 12292
  29.0 53.0 %copy-start.8 = (f32[1,128,1024]{2,0,1:T(1,128)}, f32[1,128,1024]{2,0,1:T(1,128)S(1)}, u32[]{:S(2)}) copy-start(f32[1,128,1024]{2,0,1:T(1,128)S(1)} %fusion.74) | copy-start | bytes 1572868
  29.1 41.8 %copy-start.1 = (bf16[128,1024]{1,0:T(8,128)(2,1)S(1)}, bf16[128,1024]{1,0:T(8,128)(2,1)}, u32[]{:S(2)}) copy-start(bf16[128,1024]{1,0:T(8,128)(2,1)} %param.23) | copy-start | bytes 786436
  29.1 43.8 %copy-start.39 = (s32[1024]{0:T(1024)S(1)}, s32[1024]{0:T(1024)}, u32[]{:S(2)}) copy-start(s32[1024]{0:T(1024)} %param.22) | copy-start | bytes 12292
  41.6 11.2 %collective-permute-start.2 = (bf16[128,1024]{1,0:T(8,128)(2,1)S(1)}, bf16[128,1024]{1,0:T(8,128)(2,1)S(1)}, u32[]{:S(2)}, u32[]{:S(2)}) collective-permute-start(bf16[128,1024]{1,0:T(8,128)(2,1)S(1)} %fusion.64), channel_id=1, source_target_pairs={{0,4},{4,8},{8,12},{12,16},{16,20},{20,24},{24,28},{28,0},{1,5},{5... | collective-permute-start | bytes 786440 | tf_op jit(solution)/shard_map/ppermute | solution.py:22
  52.7 9.5 %collective-permute-start.3 = (bf16[128,1024]{1,0:T(8,128)(2,1)S(1)}, bf16[128,1024]{1,0:T(8,128)(2,1)S(1)}, u32[]{:S(2)}, u32[]{:S(2)}) collective-permute-start(bf16[128,1024]{1,0:T(8,128)(2,1)S(1)} %collective-permute-done.2), channel_id=1, source_target_pairs={{0,4},{4,8},{8,12},{12,16},{16,20},{20,24},{24,28},{28,0},{1,5},{5... | collective-permute-start | bytes 786440 | tf_op jit(solution)/shard_map/ppermute | solution.py:22
  52.7 9.5 %collective-permute-start.6 = (bf16[128,1024]{1,0:T(8,128)(2,1)S(1)}, bf16[128,1024]{1,0:T(8,128)(2,1)S(1)}, u32[]{:S(2)}, u32[]{:S(2)}) collective-permute-start(bf16[128,1024]{1,0:T(8,128)(2,1)S(1)} %fusion.64), channel_id=1, source_target_pairs={{0,28},{4,0},{8,4},{12,8},{16,12},{20,16},{24,20},{28,24},{1,29},{... | collective-permute-start | bytes 786440 | tf_op jit(solution)/shard_map/ppermute | solution.py:24
  62.2 8.7 %collective-permute-start.4 = (bf16[128,1024]{1,0:T(8,128)(2,1)S(1)}, bf16[128,1024]{1,0:T(8,128)(2,1)S(1)}, u32[]{:S(2)}, u32[]{:S(2)}) collective-permute-start(bf16[128,1024]{1,0:T(8,128)(2,1)S(1)} %collective-permute-done.3), channel_id=1, source_target_pairs={{0,4},{4,8},{8,12},{12,16},{16,20},{20,24},{24,28},{28,0},{1,5},{5... | collective-permute-start | bytes 786440 | tf_op jit(solution)/shard_map/ppermute | solution.py:22
  62.2 10.7 %collective-permute-start.7 = (bf16[128,1024]{1,0:T(8,128)(2,1)S(1)}, bf16[128,1024]{1,0:T(8,128)(2,1)S(1)}, u32[]{:S(2)}, u32[]{:S(2)}) collective-permute-start(bf16[128,1024]{1,0:T(8,128)(2,1)S(1)} %collective-permute-done.6), channel_id=1, source_target_pairs={{0,28},{4,0},{8,4},{12,8},{16,12},{20,16},{24,20},{28,24},{1,29},{... | collective-permute-start | bytes 786440 | tf_op jit(solution)/shard_map/ppermute | solution.py:24
  70.8 9.1 %collective-permute-start.5 = (bf16[128,1024]{1,0:T(8,128)(2,1)S(1)}, bf16[128,1024]{1,0:T(8,128)(2,1)S(1)}, u32[]{:S(2)}, u32[]{:S(2)}) collective-permute-start(bf16[128,1024]{1,0:T(8,128)(2,1)S(1)} %collective-permute-done.4), channel_id=1, source_target_pairs={{0,4},{4,8},{8,12},{12,16},{16,20},{20,24},{24,28},{28,0},{1,5},{5... | collective-permute-start | bytes 786440 | tf_op jit(solution)/shard_map/ppermute | solution.py:22
  72.9 12.2 %collective-permute-start.8 = (bf16[128,1024]{1,0:T(8,128)(2,1)S(1)}, bf16[128,1024]{1,0:T(8,128)(2,1)S(1)}, u32[]{:S(2)}, u32[]{:S(2)}) collective-permute-start(bf16[128,1024]{1,0:T(8,128)(2,1)S(1)} %collective-permute-done.7), channel_id=1, source_target_pairs={{0,28},{4,0},{8,4},{12,8},{16,12},{20,16},{24,20},{28,24},{1,29},{... | collective-permute-start | bytes 786440 | tf_op jit(solution)/shard_map/ppermute | solution.py:24
  106.7 7.8 %copy-start.32 = (f32[128,128]{0,1:T(8,128)}, f32[128,128]{0,1:T(8,128)S(1)}, u32[]{:S(2)}) copy-start(f32[128,128]{0,1:T(8,128)S(1)} %fusion.98) | copy-start | bytes 196612
  109.2 7.4 %copy-start.27 = (f32[128,128]{0,1:T(8,128)}, f32[128,128]{0,1:T(8,128)S(1)}, u32[]{:S(2)}) copy-start(f32[128,128]{0,1:T(8,128)S(1)} %fusion.107) | copy-start | bytes 196612
  110.5 8.1 %copy-start.28 = (f32[128,128]{0,1:T(8,128)}, f32[128,128]{0,1:T(8,128)S(1)}, u32[]{:S(2)}) copy-start(f32[128,128]{0,1:T(8,128)S(1)} %fusion.110) | copy-start | bytes 196612
  111.7 6.8 %copy-start.29 = (f32[128,128]{0,1:T(8,128)}, f32[128,128]{0,1:T(8,128)S(1)}, u32[]{:S(2)}) copy-start(f32[128,128]{0,1:T(8,128)S(1)} %fusion.113) | copy-start | bytes 196612
  113.0 7.5 %copy-start.30 = (f32[128,128]{0,1:T(8,128)}, f32[128,128]{0,1:T(8,128)S(1)}, u32[]{:S(2)}) copy-start(f32[128,128]{0,1:T(8,128)S(1)} %fusion.116) | copy-start | bytes 196612
  114.3 6.2 %copy-start.31 = (f32[128,128]{0,1:T(8,128)}, f32[128,128]{0,1:T(8,128)S(1)}, u32[]{:S(2)}) copy-start(f32[128,128]{0,1:T(8,128)S(1)} %fusion.119) | copy-start | bytes 196612
  114.4 8.0 %copy-start = (bf16[8,128,1024]{2,1,0:T(8,128)(2,1)}, bf16[8,128,1024]{2,1,0:T(8,128)(2,1)S(1)}, u32[]{:S(2)}) copy-start(bf16[8,128,1024]{2,1,0:T(8,128)(2,1)S(1)} %get-tuple-element.47) | copy-start | bytes 6291460
  124.3 7.7 %copy-start.12 = (bf16[128,1024]{0,1:T(8,128)(2,1)S(1)}, bf16[128,1024]{0,1:T(8,128)(2,1)}, u32[]{:S(2)}) copy-start(bf16[128,1024]{0,1:T(8,128)(2,1)} %copy.113) | copy-start | bytes 786436
  144.9 19.5 %copy-start.10 = (bf16[1024,1024]{1,0:T(8,128)(2,1)S(1)}, bf16[1024,1024]{1,0:T(8,128)(2,1)}, u32[]{:S(2)}) copy-start(bf16[1024,1024]{1,0:T(8,128)(2,1)} %all-gather.2.cloned.1.call-done) | copy-start | bytes 6291460
  144.9 19.5 %copy-start.13 = (bf16[128,1024]{1,0:T(8,128)(2,1)S(1)}, bf16[128,1024]{1,0:T(8,128)(2,1)}, u32[]{:S(2)}) copy-start(bf16[128,1024]{1,0:T(8,128)(2,1)} %get-tuple-element.90) | copy-start | bytes 786436
  145.0 125.4 %all-reduce.3.cloned.1.call-start = ((), (), s32[]{:S(2)}) async-start(), calls=%async_computation.3 | async-start | bytes 524288 | tf_op jit(solution)/shard_map/psum | solution.py:201
  155.5 13.7 %copy-start.14 = (bf16[128,1024]{1,0:T(8,128)(2,1)S(1)}, bf16[128,1024]{1,0:T(8,128)(2,1)}, u32[]{:S(2)}) copy-start(bf16[128,1024]{1,0:T(8,128)(2,1)} %get-tuple-element.96) | copy-start | bytes 786436
  155.5 14.6 %copy-start.15 = (bf16[128,1024]{1,0:T(8,128)(2,1)S(1)}, bf16[128,1024]{1,0:T(8,128)(2,1)}, u32[]{:S(2)}) copy-start(bf16[128,1024]{1,0:T(8,128)(2,1)} %get-tuple-element.98) | copy-start | bytes 786436
  155.5 15.5 %copy-start.16 = (bf16[128,1024]{1,0:T(8,128)(2,1)S(1)}, bf16[128,1024]{1,0:T(8,128)(2,1)}, u32[]{:S(2)}) copy-start(bf16[128,1024]{1,0:T(8,128)(2,1)} %get-tuple-element.100) | copy-start | bytes 786436
  155.5 16.4 %copy-start.17 = (bf16[128,1024]{1,0:T(8,128)(2,1)S(1)}, bf16[128,1024]{1,0:T(8,128)(2,1)}, u32[]{:S(2)}) copy-start(bf16[128,1024]{1,0:T(8,128)(2,1)} %get-tuple-element.102) | copy-start | bytes 786436
  161.5 11.3 %copy-start.18 = (bf16[128,1024]{1,0:T(8,128)(2,1)S(1)}, bf16[128,1024]{1,0:T(8,128)(2,1)}, u32[]{:S(2)}) copy-start(bf16[128,1024]{1,0:T(8,128)(2,1)} %get-tuple-element.104) | copy-start | bytes 786436
  165.4 43.2 %copy-start.20 = (bf16[128,1024]{1,0:T(8,128)(2,1)S(1)}, bf16[128,1024]{1,0:T(8,128)(2,1)}, u32[]{:S(2)}) copy-start(bf16[128,1024]{1,0:T(8,128)(2,1)} %param.16) | copy-start | bytes 786436
  209.8 9.6 %copy-start.36 = (f32[128,128]{1,0:T(8,128)S(1)}, f32[128,128]{1,0:T(8,128)}, u32[]{:S(2)}) copy-start(f32[128,128]{1,0:T(8,128)} %copy.73) | copy-start | bytes 196612
  209.8 10.2 %copy-start.35 = (f32[128,128]{0,1:T(8,128)S(1)}, f32[128,128]{0,1:T(8,128)}, u32[]{:S(2)}) copy-start(f32[128,128]{0,1:T(8,128)} %get-tuple-element.88) | copy-start | bytes 196612
  216.7 7.2 %copy-start.11 = (bf16[128,2048]{1,0:T(8,128)(2,1)S(1)}, bf16[128,2048]{1,0:T(8,128)(2,1)}, u32[]{:S(2)}) copy-start(bf16[128,2048]{1,0:T(8,128)(2,1)} %reduce-scatter.2.cloned.1.call-done) | copy-start | bytes 1572868
  220.2 51.9 %collective-permute-start.9 = (bf16[127,1024]{1,0:T(8,128)(2,1)S(1)}, bf16[127,1024]{1,0:T(8,128)(2,1)S(1)}, u32[]{:S(2)}, u32[]{:S(2)}) collective-permute-start(bf16[127,1024]{1,0:T(8,128)(2,1)S(1)} %slice.308), channel_id=1, source_target_pairs={{4,0},{8,4},{12,8},{16,12},{20,16},{24,20},{28,24},{5,1},{9,5},{13... | collective-permute-start | bytes 780296 | tf_op jit(solution)/shard_map/ppermute | solution.py:46
  223.9 48.4 %copy-start.34 = (f32[128,1024]{1,0:T(8,128)S(1)}, f32[128,1024]{1,0:T(8,128)}, u32[]{:S(2)}) copy-start(f32[128,1024]{1,0:T(8,128)} %param.18) | copy-start | bytes 1572868
  272.3 5.8 %copy-start.3 = (bf16[128,1024]{1,0:T(8,128)(2,1)S(1)}, bf16[128,1024]{1,0:T(8,128)(2,1)}, u32[]{:S(2)}) copy-start(bf16[128,1024]{1,0:T(8,128)(2,1)} %copy-done.2) | copy-start | bytes 786436
  272.3 5.8 %copy-start.9 = (f32[1,128,1024]{2,0,1:T(1,128)S(1)}, f32[1,128,1024]{2,0,1:T(1,128)}, u32[]{:S(2)}) copy-start(f32[1,128,1024]{2,0,1:T(1,128)} %copy-done.8) | copy-start | bytes 1572868
  272.3 5.8 %copy-start.22 = (bf16[128,1024]{1,0:T(8,128)(2,1)S(1)}, bf16[128,1024]{1,0:T(8,128)(2,1)}, u32[]{:S(2)}) copy-start(bf16[128,1024]{1,0:T(8,128)(2,1)} %param.17) | copy-start | bytes 786436
  278.1 2.8 copy-start.24
  278.1 2.8 copy-start.7
  305.4 3.1 collective-permute-start.10
  (7 other events, 6.5 us)
Sparse Core Ops, SparseCore 0:
  21.5 30.9 all-gather.1
  145.1 50.6 reduce-scatter.1
  219.5 50.7 all-reduce.2
